TPU v7x, 256 devices: a whole 4x4x8 slice. The times are simulated.
256 devices in a mesh: dp: 8 (over x, z_lo), seq: 32 (over z_hi, y, core).
Axes of the slice: x: 4, y: 4, z: 8 (z_hi: 4, z_lo: 2; z = z_hi * 2 + z_lo), core: 2. Of those that a mesh axis runs over, the one named last changes fastest.
Arguments:
- inputs: float32 [8, 4096, 2048], P('dp', 'seq'), may hold values from -6 to 6
- cotangent: float32 [8, 4096, 2048], P('dp', 'seq'), may hold values from -6 to 6
- block_mix: float32 [128, 128], replicated, may hold values from -0.5 to 0.5
- twist_hi: float32 [2, 2, 2048], replicated, may hold values from -3 to 3
- twist_lo: float32 [2, 2, 2048], replicated, may hold values from -3 to 3
- gain: float32 [2048], replicated, may hold values from 0.5 to 1.5
- gate_up: float32 [128, 2, 16, 256], P('seq'), may hold values from -0.5 to 0.5
- down: float32 [256, 16, 128], P('seq'), may hold values from -0.375 to 0.375
Outputs:
- grad_inputs: float32 [8, 4096, 2048], P('dp', 'seq')
- grad_gate_up: float32 [128, 2, 16, 256], P('seq')
- grad_down: float32 [256, 16, 128], P('seq')
- grad_block_mix: float32 [128, 128], replicated
- grad_twist_hi: float32 [2, 2, 2048], replicated
- grad_twist_lo: float32 [2, 2, 2048], replicated
- grad_gain: float32 [2048], replicated
All inputs are finite; a program needn't handle non-finite values.
Results may differ from a plain program's by a relative error of at most 0.00022.
Values sent between devices are 32-bit elements; how exact they have to be, the bound alone decides.
No kernel may reach another device: no remote copies, remote signals or barrier semaphores. Data moves between devices by JAX's collectives and lax.ppermute only.
A program may use at most 64 MiB of HBM per device.

v0:
```python
import math
import jax
import jax.numpy as jnp
from jax import lax
from jax.sharding import PartitionSpec as P

NB = 16
BLK = 128
DB = 128
HIGH = lax.Precision.HIGHEST
EPS = 1e-05


def from_partner(block, axis, distance):
    count = lax.axis_size(axis)
    route = []
    for low in range(count):
        high = low | 1 << distance
        if high != low and high < count:
            route += [(low, high), (high, low)]
    return lax.ppermute(block, axis, route)


def side_of(bit):
    return lax.axis_index("seq") // (1 << bit) % 2


def forward_section(field, coeff, bit):
    partner = from_partner(field, "seq", bit)
    own = coeff[side_of(bit)]
    return (own[0] * field + own[1] * partner, partner)


def backward_section(grad, field, partner, coeff, bit):
    side = side_of(bit)
    own = coeff[side]
    sent = from_partner(own[1] * grad, "seq", bit)
    back = own[0] * grad + sent
    term = jnp.stack([jnp.sum(grad * field, axis=0), jnp.sum(grad * partner, axis=0)])
    pick = (jnp.arange(2) == side).astype(jnp.float32)
    return (back, pick[:, None, None] * term[None])


def exchange(x):
    return lax.all_to_all(x, "seq", 0, 0, tiled=True)


def to_blocks(field, count):
    tokens = field.shape[0]
    halves = count // NB
    x = field.reshape(halves, tokens // halves, NB, DB)
    x = jnp.transpose(x, (2, 0, 1, 3))
    return x.reshape(count, tokens // halves, DB)


def from_blocks(x, tokens, count):
    halves = count // NB
    x = x.reshape(NB, halves, tokens // halves, DB)
    x = jnp.transpose(x, (1, 2, 0, 3))
    return x.reshape(tokens, NB * DB)


def per_device(inputs, cotangent, block_mix, twist_hi, twist_lo, gain, gate_up, down):
    seq_in = inputs[0]
    tokens, width = seq_in.shape
    count = lax.axis_size("seq")
    halves = count // NB
    top_bit = count.bit_length() - 2
    nblocks = tokens // BLK
    rows_gu = gate_up.shape[0]
    rows_dn = down.shape[0]
    fb = gate_up.shape[3]
    gu_n = jnp.transpose(gate_up, (2, 0, 1, 3)).reshape(NB, rows_gu * 2 * fb)
    dn_n = jnp.transpose(down, (1, 0, 2)).reshape(NB, rows_dn * DB)
    wbuf = jnp.concatenate([gu_n, dn_n], axis=1)
    wbuf = jnp.repeat(wbuf, halves, axis=0)
    wrecv = exchange(wbuf)
    w_gu = wrecv[:, : rows_gu * 2 * fb].reshape(count * rows_gu, 2, fb)
    w_dn = wrecv[:, rows_gu * 2 * fb :].reshape(count * rows_dn, DB)
    grad_out = cotangent[0]
    cot_blk = exchange(to_blocks(grad_out, count)).reshape(-1, DB)
    xb = seq_in.reshape(nblocks, BLK, width)
    mixed = jnp.einsum("ij,kjd->kid", block_mix, xb, precision=HIGH).reshape(tokens, width)
    first, mixed_peer = forward_section(mixed, twist_hi, top_bit)
    second, first_peer = forward_section(first, twist_lo, 0)
    resid = seq_in + second
    scale = lax.rsqrt(jnp.mean(resid * resid, axis=-1, keepdims=True) + EPS)
    unit = resid * scale
    normed = unit * gain
    x_blk = exchange(to_blocks(normed, count)).reshape(-1, DB)
    gate_val = jnp.dot(x_blk, w_gu[:, 0], precision=HIGH)
    up_val = jnp.dot(x_blk, w_gu[:, 1], precision=HIGH)
    sig = jax.nn.sigmoid(gate_val)
    act = gate_val * sig
    hidden = act * up_val
    grad_hidden = jnp.dot(cot_blk, w_dn.T, precision=HIGH)
    grad_gate = grad_hidden * up_val * sig * (1.0 + gate_val * (1.0 - sig))
    grad_up = grad_hidden * act
    grad_x = jnp.dot(grad_gate, w_gu[:, 0].T, precision=HIGH) + jnp.dot(
        grad_up, w_gu[:, 1].T, precision=HIGH
    )
    grad_normed = from_blocks(exchange(grad_x.reshape(count, -1, DB)), tokens, count)
    d_gate = jnp.dot(x_blk.T, grad_gate, precision=HIGH)
    d_up = jnp.dot(x_blk.T, grad_up, precision=HIGH)
    d_gu = jnp.stack([d_gate, d_up], axis=1).reshape(count, rows_gu * 2 * fb)
    d_dn = jnp.dot(hidden.T, cot_blk, precision=HIGH).reshape(count, rows_dn * DB)
    grecv = exchange(jnp.concatenate([d_gu, d_dn], axis=1))
    grecv = grecv.reshape(NB, halves, -1).sum(axis=1)
    part_gu = jnp.transpose(grecv[:, : rows_gu * 2 * fb].reshape(NB, rows_gu, 2, fb), (1, 2, 0, 3))
    part_down = jnp.transpose(grecv[:, rows_gu * 2 * fb :].reshape(NB, rows_dn, DB), (1, 0, 2))
    part_gu, part_down = lax.psum((part_gu, part_down), "dp")
    grad_gain_local = jnp.sum(grad_normed * unit, axis=0)
    weighted = grad_normed * gain
    inner = jnp.mean(weighted * resid, axis=-1, keepdims=True)
    grad_resid = grad_out + scale * weighted - resid * scale * scale * scale * inner
    grad_first, term_lo = backward_section(grad_resid, first, first_peer, twist_lo, 0)
    grad_mixed, term_hi = backward_section(grad_first, mixed, mixed_peer, twist_hi, top_bit)
    grad_mb = grad_mixed.reshape(nblocks, BLK, width)
    term_block = jnp.einsum("kid,kjd->ij", grad_mb, xb, precision=HIGH)
    grad_seq = jnp.einsum("ij,kid->kjd", block_mix, grad_mb, precision=HIGH).reshape(tokens, width)
    grad_seq = grad_seq + grad_resid
    sum_block, sum_hi, sum_lo, sum_gain = lax.psum(
        (term_block, term_hi, term_lo, grad_gain_local), ("dp", "seq")
    )
    factor = 1.0 / math.sqrt(lax.axis_size("dp") * count * tokens)
    return (
        grad_seq[None],
        part_gu * factor,
        part_down * factor,
        sum_block * factor,
        sum_hi * factor,
        sum_lo * factor,
        sum_gain * factor,
    )


def solution(mesh):
    return jax.shard_map(
        per_device,
        mesh=mesh,
        in_specs=(
            P("dp", "seq", None),
            P("dp", "seq", None),
            P(),
            P(),
            P(),
            P(),
            P("seq", None, None, None),
            P("seq", None, None),
        ),
        out_specs=(
            P("dp", "seq", None),
            P("seq", None, None, None),
            P("seq", None, None),
            P(),
            P(),
            P(),
            P(),
        ),
        check_vma=False,
    )
```

profile of v0, /device:TPU:1, one launch (start us, length us, event | category | flops | bytes accessed | tf_op | source)
XLA Modules:
  0.0 787.0 jit_solution(7601056932142582993)
XLA Ops:
  8.8 2.3 convolution_bitcast_fusion.2
  11.2 7.8 collective-permute-start
  20.1 2.4 all_to_all.23
  22.5 6.5 all-to-all-start
  29.4 1.3 copy.50
  30.8 45.8 %all-to-all-done = f32[32,1,3072]{2,1,0:T(1,128)} async-done(((f32[32,1,3072]{2,1,0:T(1,128)}), f32[32,1,3072]{2,1,0:T(1,128)}, u32[]{:S(2)}, u32[]{:S(2)}) %all-to-all-start) | async-done | bytes 393248 | tf_op jit(solution)/shard_map/all_to_all | solution.py:45
  76.6 6.7 all-to-all-start.1
  83.9 2.4 collective-permute-done.1
  87.8 1.3 copy.51
  89.1 18.3 %all-to-all-done.1 = f32[32,64,128]{2,1,0:T(8,128)} async-done(((f32[32,64,128]{2,1,0:T(8,128)}), f32[32,64,128]{2,1,0:T(8,128)}, u32[]{:S(2)}, u32[]{:S(2)}) %all-to-all-start.1) | async-done | bytes 1048608 | tf_op jit(solution)/shard_map/all_to_all | solution.py:45
  107.4 10.3 %all-to-all-start.2 = ((f32[32,64,128]{2,1,0:T(8,128)}), f32[32,64,128]{2,1,0:T(8,128)S(1)}, u32[]{:S(2)}, u32[]{:S(2)}) async-start(f32[32,64,128]{2,1,0:T(8,128)} %bitcast.126), calls=%async_computation.2 | async-start | bytes 2097152 | tf_op jit(solution)/shard_map/all_to_all | solution.py:45
  117.7 1.1 copy.99
  120.2 1.2 reshape.129
  121.3 1.6 reshape.123
  123.8 4.5 convolution_bitcast_fusion
  128.3 13.4 %all-to-all-done.2 = f32[32,64,128]{2,1,0:T(8,128)S(1)} async-done(((f32[32,64,128]{2,1,0:T(8,128)}), f32[32,64,128]{2,1,0:T(8,128)S(1)}, u32[]{:S(2)}, u32[]{:S(2)}) %all-to-all-start.2) | async-done | bytes 1048608 | tf_op jit(solution)/shard_map/all_to_all | solution.py:45
  141.7 1.8 fusion.17
  143.6 4.0 add_multiply_fusion
  147.5 4.8 fusion.2
  152.4 3.2 convolution_bitcast_fusion.3
  155.5 1.6 reshape.135
  157.1 3.6 convolution_bitcast_fusion.4
  161.2 0.9 maximum_bitcast_fusion
  162.1 1.2 copy.60
  163.3 9.5 %all-to-all-start.4 = ((f32[32,1,3072]{2,1,0:T(1,128)}), f32[32,1,3072]{2,1,0:T(1,128)S(1)}, u32[]{:S(2)}, u32[]{:S(2)}) async-start(f32[32,1,3072]{2,1,0:T(1,128)} %copy.60), calls=%async_computation.4 | async-start | bytes 786432 | tf_op jit(solution)/shard_map/all_to_all | solution.py:45
  172.8 5.2 fusion.12
  178.1 6.2 convolution_add_fusion
  184.3 4.2 all-to-all-done.4
  189.2 5.6 all-to-all-start.3
  196.0 2.7 reduce
  198.7 2.0 reshape.136
  200.6 1.5 reduce_sum.74
  203.8 15.5 %all-to-all-done.3 = f32[32,64,128]{2,1,0:T(8,128)S(1)} async-done(((f32[32,64,128]{2,1,0:T(8,128)}), f32[32,64,128]{2,1,0:T(8,128)S(1)}, u32[]{:S(2)}, u32[]{:S(2)}) %all-to-all-start.3) | async-done | bytes 1048608 | tf_op jit(solution)/shard_map/all_to_all | solution.py:45
  220.0 1.3 fusion.5
  221.3 0.9 multiply_reduce_fusion.1
  223.1 55.9 %all-reduce.10.cloned.1.call-done = (f32[4,2,16,256]{3,1,0,2:T(2,128)}, f32[8,16,128]{2,0,1:T(8,128)}) async-done(((f32[4,2,16,256]{3,1,0,2:T(2,128)}, f32[8,16,128]{2,0,1:T(8,128)}), (f32[4,2,16,256]{3,1,0,2:T(2,128)}, f32[8,16,128]{2,0,1:T(8,128)})) %all-reduce.10.cloned.1.call-update) | async-done | bytes 196624 | tf_op jit(solution)/shard_map/psum | solution.py:111
  279.0 1.0 broadcast_multiply_fusion.2
  282.9 2.3 multiply_reduce_fusion.3
  286.0 1.1 broadcast_multiply_fusion.1
  287.1 4.6 collective-permute-start.3
  291.7 246.4 %all-reduce.8.cloned.1.call-done = (f32[2,2,2048]{2,1,0:T(2,128)}, f32[2,2,2048]{2,1,0:T(2,128)}, f32[2048]{0:T(1024)}) async-done(((f32[2,2,2048]{2,1,0:T(2,128)}, f32[2,2,2048]{2,1,0:T(2,128)}, f32[2048]{0:T(1024)}), (f32[2,2,2048]{2,1,0:T(2,128)}, f32[2,2,2048]{2,1,0:T(2,128)}, f32[2048]{0:T(1024)})) %all-reduce.8.cloned.1.call-update) | async-done | bytes 73744 | tf_op jit(solution)/shard_map/psum | solution.py:122
  538.1 1.3 broadcast_multiply_fusion.9
  539.4 1.4 broadcast_multiply_fusion.7
  540.8 1.4 broadcast_multiply_fusion.6
  542.2 2.9 fusion.6
  545.2 3.3 fusion.1
  548.5 229.4 %all-reduce.6.cloned.1.call-done = f32[128,128]{1,0:T(8,128)} async-done(((f32[128,128]{1,0:T(8,128)}), f32[128,128]{1,0:T(8,128)}) %all-reduce.6.cloned.1.call-update) | async-done | bytes 65552 | tf_op jit(solution)/shard_map/psum | solution.py:122
  777.9 1.5 broadcast_multiply_fusion.3
  (110 shorter events, 15.9 us)
Async XLA Ops:
  8.0 0.8 copy-start
  8.0 11.0 %copy-start.24 = (f32[8,16,128]{2,1,0:T(8,128)S(1)}, f32[8,16,128]{2,1,0:T(8,128)}, u32[]{:S(2)}) copy-start(f32[8,16,128]{2,1,0:T(8,128)} %param.15) | copy-start | bytes 196612
  8.0 11.0 %copy-start.15 = (f32[4,2,16,256]{3,2,1,0:T(8,128)S(1)}, f32[4,2,16,256]{3,2,1,0:T(8,128)}, u32[]{:S(2)}) copy-start(f32[4,2,16,256]{3,2,1,0:T(8,128)} %param.14) | copy-start | bytes 393220
  11.1 72.2 %copy-start.2 = (f32[128,2048]{1,0:T(8,128)}, f32[128,2048]{1,0:T(8,128)S(1)}, u32[]{:S(2)}) copy-start(f32[128,2048]{1,0:T(8,128)S(1)} %convolution_bitcast_fusion.2) | copy-start | bytes 3145732
  11.1 17.9 %copy-start.8 = (f32[1,128,2048]{2,1,0:T(8,128)S(1)}, f32[1,128,2048]{2,1,0:T(8,128)}, u32[]{:S(2)}) copy-start(f32[1,128,2048]{2,1,0:T(8,128)} %param.9) | copy-start | bytes 3145732
  11.2 72.1 %collective-permute-start = (f32[128,2048]{1,0:T(8,128)S(1)}, f32[128,2048]{1,0:T(8,128)S(1)}, u32[]{:S(2)}, u32[]{:S(2)}) collective-permute-start(f32[128,2048]{1,0:T(8,128)S(1)} %convolution_bitcast_fusion.2), channel_id=1, source_target_pairs={{0,16},{16,0},{1,17},{17,1},{2,18},{18,2},{3,19},{19,3},{4,20},{20... | collective-permute-start | bytes 3145736 | tf_op jit(solution)/shard_map/ppermute | solution.py:21
  22.5 54.1 %all-to-all-start = ((f32[32,1,3072]{2,1,0:T(1,128)}), f32[32,1,3072]{2,1,0:T(1,128)}, u32[]{:S(2)}, u32[]{:S(2)}) async-start(f32[32,1,3072]{2,1,0:T(1,128)} %all_to_all.23), calls=%async_computation | async-start | bytes 786432 | tf_op jit(solution)/shard_map/all_to_all | solution.py:45
  29.3 1.4 copy-start.25
  29.3 1.4 copy-start.26
  30.7 52.7 %copy-start.18 = (f32[1,1,2048]{2,1,0:T(1,128)}, f32[1,1,2048]{2,1,0:T(1,128)S(1)}, u32[]{:S(2)}) copy-start(f32[1,1,2048]{2,1,0:T(1,128)S(1)} %get-tuple-element.51) | copy-start | bytes 24580
  30.7 55.5 %copy-start.20 = (f32[1,1,2048]{2,1,0:T(1,128)}, f32[1,1,2048]{2,1,0:T(1,128)S(1)}, u32[]{:S(2)}) copy-start(f32[1,1,2048]{2,1,0:T(1,128)S(1)} %get-tuple-element.45) | copy-start | bytes 24580
  30.8 55.5 %copy-start.22 = (f32[1,1,2048]{2,1,0:T(1,128)}, f32[1,1,2048]{2,1,0:T(1,128)S(1)}, u32[]{:S(2)}) copy-start(f32[1,1,2048]{2,1,0:T(1,128)S(1)} %get-tuple-element.46) | copy-start | bytes 24580
  76.6 30.8 %all-to-all-start.1 = ((f32[32,64,128]{2,1,0:T(8,128)}), f32[32,64,128]{2,1,0:T(8,128)}, u32[]{:S(2)}, u32[]{:S(2)}) async-start(f32[32,64,128]{2,1,0:T(8,128)} %bitcast.14), calls=%async_computation.1 | async-start | bytes 2097152 | tf_op jit(solution)/shard_map/all_to_all | solution.py:45
  83.3 3.0 copy-start.1
  83.3 3.4 copy-start.5
  83.5 3.2 copy-start.3
  83.5 2.7 collective-permute-start.1
  86.2 1.0 copy-start.6
  86.3 1.0 copy-start.17
  87.3 0.5 copy-start.27
  107.4 34.3 %all-to-all-start.2 = ((f32[32,64,128]{2,1,0:T(8,128)}), f32[32,64,128]{2,1,0:T(8,128)S(1)}, u32[]{:S(2)}, u32[]{:S(2)}) async-start(f32[32,64,128]{2,1,0:T(8,128)} %bitcast.126), calls=%async_computation.2 | async-start | bytes 2097152 | tf_op jit(solution)/shard_map/all_to_all | solution.py:45
  123.8 17.9 %copy-start.13 = (f32[128,1,256]{2,1,0:T(1,128)S(1)}, f32[128,1,256]{2,1,0:T(1,128)}, u32[]{:S(2)}) copy-start(f32[128,1,256]{2,1,0:T(1,128)} %get-tuple-element.43) | copy-start | bytes 393220
  128.3 15.2 %copy-start.14 = (f32[128,1,256]{2,1,0:T(1,128)S(1)}, f32[128,1,256]{2,1,0:T(1,128)}, u32[]{:S(2)}) copy-start(f32[128,1,256]{2,1,0:T(1,128)} %get-tuple-element.44) | copy-start | bytes 393220
  141.7 1.9 copy-start.10
  147.5 4.9 copy-start.31
  157.1 3.6 copy-start.16
  163.3 25.2 %all-to-all-start.4 = ((f32[32,1,3072]{2,1,0:T(1,128)}), f32[32,1,3072]{2,1,0:T(1,128)S(1)}, u32[]{:S(2)}, u32[]{:S(2)}) async-start(f32[32,1,3072]{2,1,0:T(1,128)} %copy.60), calls=%async_computation.4 | async-start | bytes 786432 | tf_op jit(solution)/shard_map/all_to_all | solution.py:45
  172.8 5.3 copy-start.11
  188.5 0.7 copy-start.12
  189.2 30.1 %all-to-all-start.3 = ((f32[32,64,128]{2,1,0:T(8,128)}), f32[32,64,128]{2,1,0:T(8,128)S(1)}, u32[]{:S(2)}, u32[]{:S(2)}) async-start(f32[32,64,128]{2,1,0:T(8,128)} %bitcast.132), calls=%async_computation.3 | async-start | bytes 2097152 | tf_op jit(solution)/shard_map/all_to_all | solution.py:45
  194.9 84.2 %all-reduce.10.cloned.1.call-start = ((), (), s32[]{:S(2)}) async-start(), calls=%async_computation.7 | async-start | bytes 393216 | tf_op jit(solution)/shard_map/psum | solution.py:111
  202.9 17.1 %copy-start.28 = (f32[128]{0:T(128)S(1)}, f32[128]{0:T(128)}, u32[]{:S(2)}) copy-start(f32[128]{0:T(128)} %copy-done.27) | copy-start | bytes 1540
  203.5 334.6 %all-reduce.8.cloned.1.call-start = ((), (), s32[]{:S(2)}) async-start(), calls=%async_computation.6 | async-start | bytes 147456 | tf_op jit(solution)/shard_map/psum | solution.py:122
  219.3 1.9 copy-start.4
  219.3 1.9 copy-start.7
  219.3 1.9 copy-start.9
  221.3 0.9 copy-start.23
  222.2 60.1 %copy-start.30 = (f32[2]{0:T(128)S(1)}, f32[2]{0:T(128)}, u32[]{:S(2)}) copy-start(f32[2]{0:T(128)} %compare_convert_fusion) | copy-start | bytes 28
  222.2 60.8 %copy-start.21 = (f32[1,1,2048]{2,1,0:T(1,128)S(1)}, f32[1,1,2048]{2,1,0:T(1,128)}, u32[]{:S(2)}) copy-start(f32[1,1,2048]{2,1,0:T(1,128)} %copy-done.20) | copy-start | bytes 24580
  222.3 60.6 %collective-permute-start.2 = (f32[128,2048]{1,0:T(8,128)S(1)}, f32[128,2048]{1,0:T(8,128)}, u32[]{:S(2)}, u32[]{:S(2)}) collective-permute-start(f32[128,2048]{1,0:T(8,128)S(1)} %broadcast_multiply_fusion), channel_id=1, source_target_pairs={{0,1},{1,0},{2,3},{3,2},{4,5},{5,4},{6,7},{7,6},{8,9},{9,8},{10,11... | collective-permute-start | bytes 3145736 | tf_op jit(solution)/shard_map/ppermute | solution.py:21
  282.9 2.3 copy-start.29
  282.9 3.1 copy-start.19
  286.0 491.9 %all-reduce.6.cloned.1.call-start = ((), (), s32[]{:S(2)}) async-start(), calls=%async_computation.5 | async-start | bytes 131072 | tf_op jit(solution)/shard_map/psum | solution.py:122
  287.1 255.1 %collective-permute-start.3 = (f32[128,2048]{1,0:T(8,128)}, f32[128,2048]{1,0:T(8,128)}, u32[]{:S(2)}, u32[]{:S(2)}) collective-permute-start(f32[128,2048]{1,0:T(8,128)} %broadcast_multiply_fusion.1), channel_id=1, source_target_pairs={{0,16},{16,0},{1,17},{17,1},{2,18},{18,2},{3,19},{19,3},{4,20},{20... | collective-permute-start | bytes 3145736 | tf_op jit(solution)/shard_map/ppermute | solution.py:21
Sparse Core Ops, SparseCore 0:
  203.7 75.3 all-reduce.9
Sparse Core Ops, SparseCore 1:
  286.0 252.0 all-reduce.7
  545.2 232.6 all-reduce.5
where the time goes:
time: 794 us; the launch traced here: 787 us
  waiting for transfers between devices  631 us (79%)
  starting transfers between devices  52.6 us (7%)
  matrix products  41.9 us (5%)
  local copies, waits for them, and re-layouts  23.6 us (3%)
  other arithmetic  21.3 us (3%)
  between operations  16.3 us (2%)
    psum x2, waiting for transfers between devices, per_device(): lax.psum((term_block, term_hi, term_lo, grad_gain_local), ('dp', 'seq'))  476 us
    all_to_all x5, waiting for transfers between devices, exchange(): return lax.all_to_all(x, 'seq', 0, 0, tiled=True)  97.2 us
    psum x1, waiting for transfers between devices, per_device(): part_gu, part_down = lax.psum((part_gu, part_down), 'dp')  55.9 us
    all_to_all x5, starting transfers between devices, exchange(): return lax.all_to_all(x, 'seq', 0, 0, tiled=True)  38.6 us
  transfers between devices with their start and end apart: 12, of which 9 were waited for; matrix products, arithmetic and copies ran while one was open for 6% of the time, Pallas kernels for 0%

commit v1 on v0

--- a/solution.py
+++ b/solution.py
@@ -120,7 +120,7 @@
     grad_seq = jnp.einsum("ij,kid->kjd", block_mix, grad_mb, precision=HIGH).reshape(tokens, width)
     grad_seq = grad_seq + grad_resid
     sum_block, sum_hi, sum_lo, sum_gain = lax.psum(
-        (term_block, term_hi, term_lo, grad_gain_local), ("dp", "seq")
+        lax.psum((term_block, term_hi, term_lo, grad_gain_local), "seq"), "dp"
     )
     factor = 1.0 / math.sqrt(lax.axis_size("dp") * count * tokens)
     return (

time: 794 us -> 917 us (1.15)
  waiting for transfers between devices: 631 us -> 750 us
    psum x2 -> x3, waiting for transfers between devices: 476 us -> 581 us  [the longest x2 514 us: per_device(): lax.psum((term_block, term_hi, term_lo, grad_gain_local), 'seq')]
    psum x1, waiting for transfers between devices: 55.9 us -> 71.6 us  [per_device(): part_gu, part_down = lax.psum((part_gu, part_down), 'dp')]
  transfers between devices with their start and end apart: 12 -> 13, of which waited for: 9 -> 10; matrix products, arithmetic and copies ran while one was open for 6% -> 6% of each run, Pallas kernels for 0% -> 0%
where the time goes in v1:
time: 917 us; the launch traced here: 906 us
  waiting for transfers between devices  750 us (82%)
  starting transfers between devices  57.5 us (6%)
  matrix products  38.1 us (4%)
  local copies, waits for them, and re-layouts  27.2 us (3%)
  other arithmetic  18.8 us (2%)
  between operations  14.5 us (2%)
    psum x2, waiting for transfers between devices, per_device(): lax.psum((term_block, term_hi, term_lo, grad_gain_local), 'seq')  514 us
    all_to_all x5, waiting for transfers between devices, exchange(): return lax.all_to_all(x, 'seq', 0, 0, tiled=True)  95.1 us
    psum x1, waiting for transfers between devices, per_device(): part_gu, part_down = lax.psum((part_gu, part_down), 'dp')  71.6 us
    psum x1, waiting for transfers between devices, per_device(): lax.psum(lax.psum((term_block, term_hi, term_lo, grad_gain_local), 'seq')...  66.9 us
    all_to_all x5, starting transfers between devices, exchange(): return lax.all_to_all(x, 'seq', 0, 0, tiled=True)  42.8 us
  transfers between devices with their start and end apart: 13, of which 10 were waited for; matrix products, arithmetic and copies ran while one was open for 6% of the time, Pallas kernels for 0%

profile of v1, /device:TPU:1, one launch (start us, length us, event | category | flops | bytes accessed | tf_op | source)
XLA Modules:
  0.0 905.9 jit_solution(9122463818548406592)
XLA Ops:
  8.0 2.3 convolution_bitcast_fusion.2
  10.3 7.8 collective-permute-start
  19.3 2.4 all_to_all.23
  21.7 6.5 all-to-all-start
  28.6 1.3 copy.50
  29.9 45.8 %all-to-all-done = f32[32,1,3072]{2,1,0:T(1,128)} async-done(((f32[32,1,3072]{2,1,0:T(1,128)}), f32[32,1,3072]{2,1,0:T(1,128)}, u32[]{:S(2)}, u32[]{:S(2)}) %all-to-all-start) | async-done | bytes 393248 | tf_op jit(solution)/shard_map/all_to_all | solution.py:45
  75.8 6.7 all-to-all-start.1
  83.0 2.4 collective-permute-done.1
  86.7 1.3 copy.51
  88.0 18.5 %all-to-all-done.1 = f32[32,64,128]{2,1,0:T(8,128)} async-done(((f32[32,64,128]{2,1,0:T(8,128)}), f32[32,64,128]{2,1,0:T(8,128)}, u32[]{:S(2)}, u32[]{:S(2)}) %all-to-all-start.1) | async-done | bytes 1048608 | tf_op jit(solution)/shard_map/all_to_all | solution.py:45
  106.5 10.3 %all-to-all-start.2 = ((f32[32,64,128]{2,1,0:T(8,128)}), f32[32,64,128]{2,1,0:T(8,128)S(1)}, u32[]{:S(2)}, u32[]{:S(2)}) async-start(f32[32,64,128]{2,1,0:T(8,128)} %bitcast.125), calls=%async_computation.2 | async-start | bytes 2097152 | tf_op jit(solution)/shard_map/all_to_all | solution.py:45
  116.9 1.1 copy.99
  119.3 1.2 reshape.129
  120.5 1.6 reshape.123
  123.0 4.5 convolution_bitcast_fusion
  127.5 13.4 %all-to-all-done.2 = f32[32,64,128]{2,1,0:T(8,128)S(1)} async-done(((f32[32,64,128]{2,1,0:T(8,128)}), f32[32,64,128]{2,1,0:T(8,128)S(1)}, u32[]{:S(2)}, u32[]{:S(2)}) %all-to-all-start.2) | async-done | bytes 1048608 | tf_op jit(solution)/shard_map/all_to_all | solution.py:45
  140.9 1.8 fusion.17
  142.7 2.6 add_multiply_fusion
  145.3 3.6 fusion.12
  149.0 4.8 convolution_add_fusion
  153.7 9.5 %all-to-all-start.3 = ((f32[32,64,128]{2,1,0:T(8,128)}), f32[32,64,128]{2,1,0:T(8,128)}, u32[]{:S(2)}, u32[]{:S(2)}) async-start(f32[32,64,128]{2,1,0:T(8,128)} %bitcast.131), calls=%async_computation.3 | async-start | bytes 2097152 | tf_op jit(solution)/shard_map/all_to_all | solution.py:45
  163.3 4.2 convolution_bitcast_fusion.4
  167.5 4.9 fusion.2
  172.4 3.2 convolution_bitcast_fusion.3
  175.6 11.8 %all-to-all-done.3 = f32[32,64,128]{2,1,0:T(8,128)} async-done(((f32[32,64,128]{2,1,0:T(8,128)}), f32[32,64,128]{2,1,0:T(8,128)}, u32[]{:S(2)}, u32[]{:S(2)}) %all-to-all-start.3) | async-done | bytes 1048608 | tf_op jit(solution)/shard_map/all_to_all | solution.py:45
  187.4 2.0 copy.56
  189.4 1.3 fusion.5
  192.7 1.6 reshape.135
  195.2 1.2 reshape.134
  197.3 1.2 copy.60
  198.5 9.8 %all-to-all-start.4 = ((f32[32,1,3072]{2,1,0:T(1,128)}), f32[32,1,3072]{2,1,0:T(1,128)}, u32[]{:S(2)}, u32[]{:S(2)}) async-start(f32[32,1,3072]{2,1,0:T(1,128)} %copy.60), calls=%async_computation.4 | async-start | bytes 786432 | tf_op jit(solution)/shard_map/all_to_all | solution.py:45
  209.0 2.2 multiply_reduce_fusion.3
  211.3 1.1 broadcast_multiply_fusion.1
  212.3 5.3 collective-permute-start.3
  218.4 5.6 all-to-all-done.4
  224.0 2.7 reduce
  226.7 2.0 reshape.136
  228.6 1.5 reduce_sum.74
  230.1 260.0 %all-reduce.10.cloned.1.call-done = (f32[2,2,2048]{2,1,0:T(2,128)}, f32[2,2,2048]{2,1,0:T(2,128)}, f32[2048]{0:T(1024)}) async-done(((f32[2,2,2048]{2,1,0:T(2,128)}, f32[2,2,2048]{2,1,0:T(2,128)}, f32[2048]{0:T(1024)}), (f32[2,2,2048]{2,1,0:T(2,128)}, f32[2,2,2048]{2,1,0:T(2,128)}, f32[2048]{0:T(1024)})) %all-reduce.10.cloned.1.call-update) | async-done | bytes 73744 | tf_op jit(solution)/shard_map/psum | solution.py:123
  491.7 1.5 copy.74
  493.1 66.9 %all-reduce.12.cloned.1.call-done = (f32[2,2,2048]{2,1,0:T(2,128)}, f32[2,2,2048]{2,1,0:T(2,128)}, f32[2048]{0:T(1024)}) async-done(((f32[2,2,2048]{2,1,0:T(2,128)}, f32[2,2,2048]{2,1,0:T(2,128)}, f32[2048]{0:T(1024)}), (f32[2,2,2048]{2,1,0:T(2,128)}, f32[2,2,2048]{2,1,0:T(2,128)}, f32[2048]{0:T(1024)})) %all-reduce.12.cloned.1.call-update) | async-done | bytes 73744 | tf_op jit(solution)/shard_map/psum | solution.py:122
  560.0 1.4 broadcast_multiply_fusion.7
  561.4 2.9 fusion.6
  565.0 253.9 %all-reduce.8.cloned.1.call-done = f32[128,128]{1,0:T(8,128)} async-done(((f32[128,128]{1,0:T(8,128)}), f32[128,128]{1,0:T(8,128)}) %all-reduce.8.cloned.1.call-update) | async-done | bytes 65552 | tf_op jit(solution)/shard_map/psum | solution.py:123
  819.6 3.3 fusion.1
  822.9 71.6 %all-reduce.14.cloned.1.call-done = (f32[4,2,16,256]{3,1,0,2:T(2,128)}, f32[8,16,128]{2,0,1:T(8,128)}, f32[128,128]{1,0:T(8,128)}) async-done(((f32[4,2,16,256]{3,1,0,2:T(2,128)}, f32[8,16,128]{2,0,1:T(8,128)}, f32[128,128]{1,0:T(8,128)}), (f32[4,2,16,256]{3,1,0,2:T(2,128)}, f32[8,16,128]{2,0,1:T(8,128)}, f32[128,128]{1,0:T(8,128)})) %all-reduce.14.cloned.1.call-update) | async-done | bytes 262160 | tf_op jit(solution)/shard_map/psum | solution.py:111
  894.5 1.0 broadcast_multiply_fusion.2
  897.7 1.5 broadcast_multiply_fusion.3
  (105 shorter events, 16.8 us)
Async XLA Ops:
  7.2 0.8 copy-start
  7.2 11.0 %copy-start.21 = (f32[8,16,128]{2,1,0:T(8,128)S(1)}, f32[8,16,128]{2,1,0:T(8,128)}, u32[]{:S(2)}) copy-start(f32[8,16,128]{2,1,0:T(8,128)} %param.15) | copy-start | bytes 196612
  7.2 11.0 %copy-start.18 = (f32[4,2,16,256]{3,2,1,0:T(8,128)S(1)}, f32[4,2,16,256]{3,2,1,0:T(8,128)}, u32[]{:S(2)}) copy-start(f32[4,2,16,256]{3,2,1,0:T(8,128)} %param.14) | copy-start | bytes 393220
  10.3 72.2 %copy-start.2 = (f32[128,2048]{1,0:T(8,128)}, f32[128,2048]{1,0:T(8,128)S(1)}, u32[]{:S(2)}) copy-start(f32[128,2048]{1,0:T(8,128)S(1)} %convolution_bitcast_fusion.2) | copy-start | bytes 3145732
  10.3 17.9 %copy-start.9 = (f32[1,128,2048]{2,1,0:T(8,128)S(1)}, f32[1,128,2048]{2,1,0:T(8,128)}, u32[]{:S(2)}) copy-start(f32[1,128,2048]{2,1,0:T(8,128)} %param.9) | copy-start | bytes 3145732
  10.3 72.1 %collective-permute-start = (f32[128,2048]{1,0:T(8,128)S(1)}, f32[128,2048]{1,0:T(8,128)S(1)}, u32[]{:S(2)}, u32[]{:S(2)}) collective-permute-start(f32[128,2048]{1,0:T(8,128)S(1)} %convolution_bitcast_fusion.2), channel_id=1, source_target_pairs={{0,16},{16,0},{1,17},{17,1},{2,18},{18,2},{3,19},{19,3},{4,20},{20... | collective-permute-start | bytes 3145736 | tf_op jit(solution)/shard_map/ppermute | solution.py:21
  21.7 54.1 %all-to-all-start = ((f32[32,1,3072]{2,1,0:T(1,128)}), f32[32,1,3072]{2,1,0:T(1,128)}, u32[]{:S(2)}, u32[]{:S(2)}) async-start(f32[32,1,3072]{2,1,0:T(1,128)} %all_to_all.23), calls=%async_computation | async-start | bytes 786432 | tf_op jit(solution)/shard_map/all_to_all | solution.py:45
  28.5 1.4 copy-start.24
  28.5 1.4 copy-start.25
  75.8 30.8 %all-to-all-start.1 = ((f32[32,64,128]{2,1,0:T(8,128)}), f32[32,64,128]{2,1,0:T(8,128)}, u32[]{:S(2)}, u32[]{:S(2)}) async-start(f32[32,64,128]{2,1,0:T(8,128)} %bitcast.14), calls=%async_computation.1 | async-start | bytes 2097152 | tf_op jit(solution)/shard_map/all_to_all | solution.py:45
  82.4 3.0 copy-start.1
  82.5 2.9 copy-start.6
  82.6 3.2 copy-start.3
  82.7 2.7 collective-permute-start.1
  85.4 1.0 copy-start.7
  85.4 1.0 copy-start.20
  106.5 34.3 %all-to-all-start.2 = ((f32[32,64,128]{2,1,0:T(8,128)}), f32[32,64,128]{2,1,0:T(8,128)S(1)}, u32[]{:S(2)}, u32[]{:S(2)}) async-start(f32[32,64,128]{2,1,0:T(8,128)} %bitcast.125), calls=%async_computation.2 | async-start | bytes 2097152 | tf_op jit(solution)/shard_map/all_to_all | solution.py:45
  123.0 17.9 %copy-start.16 = (f32[128,1,256]{2,1,0:T(1,128)S(1)}, f32[128,1,256]{2,1,0:T(1,128)}, u32[]{:S(2)}) copy-start(f32[128,1,256]{2,1,0:T(1,128)} %get-tuple-element.47) | copy-start | bytes 393220
  127.5 15.2 %copy-start.17 = (f32[128,1,256]{2,1,0:T(1,128)S(1)}, f32[128,1,256]{2,1,0:T(1,128)}, u32[]{:S(2)}) copy-start(f32[128,1,256]{2,1,0:T(1,128)} %get-tuple-element.48) | copy-start | bytes 393220
  140.9 1.9 copy-start.11
  142.7 2.6 copy-start.13
  145.3 8.4 copy-start.5
  145.3 8.4 copy-start.26
  153.7 33.7 %all-to-all-start.3 = ((f32[32,64,128]{2,1,0:T(8,128)}), f32[32,64,128]{2,1,0:T(8,128)}, u32[]{:S(2)}, u32[]{:S(2)}) async-start(f32[32,64,128]{2,1,0:T(8,128)} %bitcast.131), calls=%async_computation.3 | async-start | bytes 2097152 | tf_op jit(solution)/shard_map/all_to_all | solution.py:45
  163.3 4.2 copy-start.14
  167.5 4.9 copy-start.12
  167.5 4.9 copy-start.27
  187.4 3.3 copy-start.4
  187.4 3.3 copy-start.8
  187.4 3.3 copy-start.10
  191.6 1.1 copy-start.15
  191.6 1.1 copy-start.19
  191.7 17.3 %collective-permute-start.2 = (f32[128,2048]{1,0:T(8,128)S(1)}, f32[128,2048]{1,0:T(8,128)}, u32[]{:S(2)}, u32[]{:S(2)}) collective-permute-start(f32[128,2048]{1,0:T(8,128)S(1)} %broadcast_multiply_fusion), channel_id=1, source_target_pairs={{0,1},{1,0},{2,3},{3,2},{4,5},{5,4},{6,7},{7,6},{8,9},{9,8},{10,11... | collective-permute-start | bytes 3145736 | tf_op jit(solution)/shard_map/ppermute | solution.py:21
  198.5 25.5 %all-to-all-start.4 = ((f32[32,1,3072]{2,1,0:T(1,128)}), f32[32,1,3072]{2,1,0:T(1,128)}, u32[]{:S(2)}, u32[]{:S(2)}) async-start(f32[32,1,3072]{2,1,0:T(1,128)} %copy.60), calls=%async_computation.4 | async-start | bytes 786432 | tf_op jit(solution)/shard_map/all_to_all | solution.py:45
  208.3 281.9 %all-reduce.10.cloned.1.call-start = ((), (), s32[]{:S(2)}) async-start(), calls=%async_computation.6 | async-start | bytes 147456 | tf_op jit(solution)/shard_map/psum | solution.py:123
  212.3 349.1 %collective-permute-start.3 = (f32[128,2048]{1,0:T(8,128)}, f32[128,2048]{1,0:T(8,128)}, u32[]{:S(2)}, u32[]{:S(2)}) collective-permute-start(f32[128,2048]{1,0:T(8,128)} %broadcast_multiply_fusion.1), channel_id=1, source_target_pairs={{0,16},{16,0},{1,17},{17,1},{2,18},{18,2},{3,19},{19,3},{4,20},{20... | collective-permute-start | bytes 3145736 | tf_op jit(solution)/shard_map/ppermute | solution.py:21
  218.4 341.6 %all-reduce.12.cloned.1.call-start = ((), (), s32[]{:S(2)}) async-start(), calls=%async_computation.7 | async-start | bytes 147456 | tf_op jit(solution)/shard_map/psum | solution.py:122
  490.2 328.7 %all-reduce.8.cloned.1.call-start = ((), (), s32[]{:S(2)}) async-start(), calls=%async_computation.5 | async-start | bytes 131072 | tf_op jit(solution)/shard_map/psum | solution.py:123
  560.0 4.4 copy-start.22
  560.0 258.9 %copy-start.23 = (f32[2048]{0:T(1024)S(1)}, f32[2048]{0:T(1024)}, u32[]{:S(2)}) copy-start(f32[2048]{0:T(1024)} %get-tuple-element.39) | copy-start | bytes 24580
  564.4 330.2 %all-reduce.14.cloned.1.call-start = ((), (), s32[]{:S(2)}) async-start(), calls=%async_computation.8 | async-start | bytes 524288 | tf_op jit(solution)/shard_map/psum | solution.py:111
Sparse Core Ops, SparseCore 0:
  218.5 271.6 all-reduce.9
  493.2 66.7 all-reduce.11
  564.5 254.4 all-reduce.7
  822.4 72.1 all-reduce.13
